TPU v7x, 256 devices: a whole 4x4x8 slice. The times are simulated.
256 devices in a mesh: dp: 32 (over x, y, core), tensor: 8 (over z).
Axes of the slice: x: 4, y: 4, z: 8, core: 2. Of those that a mesh axis runs over, the one named last changes fastest.
Arguments:
- hidden_states: bfloat16 [24576, 4096], P('dp', 'tensor')
- neighbour_ids: int32 [384, 2], P('dp'), may hold values from 0 to 511, as said below
- database: bfloat16 [512, 128, 896], P('dp')
- w_up: bfloat16 [896, 3584], P(None, 'tensor'), may hold values from -0.1875 to 0.1875
- w_down: bfloat16 [3584, 896], P('tensor'), may hold values from -0.09375 to 0.09375
- w_query: bfloat16 [4096, 4096], P(None, 'tensor'), may hold values from -0.09375 to 0.09375
- w_key: bfloat16 [896, 4096], P(None, 'tensor'), may hold values from -0.1875 to 0.1875
- w_value: bfloat16 [896, 4096], P(None, 'tensor'), may hold values from -0.1875 to 0.1875
Outputs:
- attended: bfloat16 [24576, 4096], P('dp', 'tensor')
Inputs may be any that keep to these rules, and one draw needn't show every extreme that they name: `neighbour_ids`: block ids are grouped by owner: index s of dp holds blocks s * 16 to (s + 1) * 16 - 1. Among the 24 ids of one sequence, no owner's blocks are named more than 2 times; one owner, the same for every sequence, is named exactly 2 times by each.
All inputs are finite; a program needn't handle non-finite values.
Results may differ from a plain program's by a relative error of at most 0.02.
Values may be sent and summed in bfloat16 or wider, within the bound.
No kernel may reach another device: no remote copies, remote signals or barrier semaphores. Data moves between devices by JAX's collectives and lax.ppermute only.
A program may use at most 128 MiB of HBM per device.

v0:
```python
import math
import jax
import jax.numpy as jnp
from jax import lax
from jax.sharding import PartitionSpec as P

HD = 128
SPAN = 64
KN = 2
NTOK = 128
EPSILON = 1e-06
LOGIT_SCALE = 3.0


def head_norm(projected):
    shaped = projected.reshape(projected.shape[0], -1, HD)
    scaled = shaped * lax.rsqrt(jnp.mean(shaped * shaped, axis=-1, keepdims=True) + EPSILON)
    return scaled.astype(jnp.bfloat16)


def attend(queries, keys, values):
    seq_rows = queries.shape[0]
    heads_here = queries.shape[1]
    span_count = seq_rows // SPAN
    shifted = jnp.concatenate(
        [queries[SPAN - 1 :], jnp.zeros((SPAN - 1, heads_here, HD), jnp.bfloat16)], axis=0
    )
    windows = shifted.reshape(span_count, SPAN, heads_here, HD)
    key_blocks = keys.reshape(span_count, KN * NTOK, heads_here, HD)
    value_blocks = values.reshape(span_count, KN * NTOK, heads_here, HD)
    scores = jnp.einsum("cqhd,ckhd->chqk", windows, key_blocks, preferred_element_type=jnp.float32)
    scores = scores * (LOGIT_SCALE / math.sqrt(HD))
    expo = jnp.exp(scores)
    weights = (expo / jnp.sum(expo, axis=-1, keepdims=True)).astype(jnp.bfloat16)
    mixed = jnp.einsum("chqk,ckhd->cqhd", weights, value_blocks, preferred_element_type=jnp.float32)
    mixed = mixed.astype(jnp.bfloat16).reshape(seq_rows, heads_here * HD)
    leading = jnp.zeros((SPAN - 1, heads_here * HD), jnp.bfloat16)
    return jnp.concatenate([leading, mixed[: seq_rows - SPAN + 1]], axis=0)


def shards(hidden_states, neighbour_ids, database, w_up, w_down, w_query, w_key, w_value):
    dp_count = lax.axis_size("dp")
    tensor_count = lax.axis_size("tensor")
    shard_blocks = database.shape[0]
    block_tokens = database.shape[1]
    enc_width = database.shape[2]
    flat_ids = neighbour_ids.reshape(-1)
    request_count = flat_ids.shape[0]
    capacity = max(2, (request_count + dp_count - 1) // dp_count + 1)
    owners = flat_ids // shard_blocks
    local_rows = flat_ids % shard_blocks
    owner_match = (owners[:, None] == jnp.arange(dp_count, dtype=jnp.int32)[None, :]).astype(
        jnp.int32
    )
    positions = jnp.arange(request_count, dtype=jnp.int32)
    earlier = (positions[:, None] > positions[None, :]).astype(jnp.int32)
    ranks = jnp.sum(jnp.dot(earlier, owner_match) * owner_match, axis=1)
    slots = owners * capacity + ranks
    slot_match = slots[None, :] == jnp.arange(dp_count * capacity, dtype=jnp.int32)[:, None]
    requests = jnp.sum(jnp.where(slot_match, local_rows[None, :], 0), axis=1)
    requests = requests.reshape(dp_count, capacity)
    replies = lax.all_to_all(
        database[lax.all_to_all(requests, "dp", split_axis=0, concat_axis=0, tiled=True)],
        "dp",
        split_axis=0,
        concat_axis=0,
        tiled=True,
    )
    raw_blocks = replies.reshape(dp_count * capacity, block_tokens, enc_width)[slots]
    raw_float = raw_blocks.astype(jnp.float32)
    normed = (
        raw_float * lax.rsqrt(jnp.mean(raw_float * raw_float, axis=-1, keepdims=True) + EPSILON)
    ).astype(jnp.bfloat16)
    own_blocks = request_count // tensor_count
    inner = jnp.einsum("bte,ef->btf", normed, w_up, preferred_element_type=jnp.float32)
    active = jax.nn.gelu(inner).astype(jnp.bfloat16)
    summed = lax.psum_scatter(
        jnp.einsum("btf,fe->bte", active, w_down, preferred_element_type=jnp.float32).astype(
            jnp.bfloat16
        ),
        "tensor",
        scatter_dimension=0,
        tiled=True,
    ).astype(jnp.float32)
    raw_own = lax.dynamic_slice_in_dim(
        raw_float, lax.axis_index("tensor") * own_blocks, own_blocks, 0
    )
    encoded_own = (raw_own + summed).astype(jnp.bfloat16)
    encoded = lax.all_gather(encoded_own, "tensor", axis=0, tiled=True)
    projected = jnp.dot(
        lax.all_gather(hidden_states, "tensor", axis=1, tiled=True),
        w_query,
        preferred_element_type=jnp.float32,
    )
    queries = head_norm(projected)
    flat_encoded = encoded.reshape(-1, enc_width)
    keys = head_norm(jnp.dot(flat_encoded, w_key, preferred_element_type=jnp.float32))
    values = jnp.dot(flat_encoded, w_value, preferred_element_type=jnp.float32).astype(jnp.bfloat16)
    values = values.reshape(flat_encoded.shape[0], -1, HD)
    return attend(queries, keys, values)


def solution(mesh):
    in_specs = (
        P("dp", "tensor"),
        P("dp", None),
        P("dp", None, None),
        P(None, "tensor"),
        P("tensor", None),
        P(None, "tensor"),
        P(None, "tensor"),
        P(None, "tensor"),
    )
    out_specs = P("dp", "tensor")
    return jax.shard_map(shards, mesh=mesh, in_specs=in_specs, out_specs=out_specs, check_vma=False)
```

profile of v0, /device:TPU:1, one launch (start us, length us, event | category | flops | bytes accessed | tf_op | source)
XLA Modules:
  0.0 541.9 jit_solution(13727991307017011752)
XLA Ops:
  6.5 0.8 copy.37
  8.0 15.3 %all_to_all.17 = s32[32,1,2]{2,1,0:T(1,128)S(1)} all-to-all(s32[32,1,2]{2,1,0:T(1,128)S(1)} %bitcast.50), channel_id=1, replica_groups=mesh['dp'=32,'tensor'=8] {'dp'}, dimensions={0} | all-to-all | bytes 512 | tf_op jit(solution)/shard_map/all_to_all | solution.py:63
  23.7 10.0 %gather_fusion = bf16[64,128,896]{2,1,0:T(8,128)(2,1)} fusion(bf16[16,128,896]{2,1,0:T(8,128)(2,1)} %param.10, s32[1024]{0:T(1024)S(1)} %pad_clamp_fusion.1), kind=kCustom, calls=%fused_computation | custom fusion | bytes 29360384 | tf_op jit(solution)/shard_map/gather | solution.py:63
  33.7 5.4 %all-to-all-start.1 = ((bf16[32,2,128,896]{3,2,1,0:T(8,128)(2,1)}), bf16[32,2,128,896]{3,2,1,0:T(8,128)(2,1)}, u32[]{:S(2)}, u32[]{:S(2)}) async-start(bf16[32,2,128,896]{3,2,1,0:T(8,128)(2,1)} %bitcast.42), calls=%async_computation.1 | async-start | bytes 29360128 | tf_op jit(solution)/shard_map/all_to_all | solution.py:62
  39.3 202.2 %all-to-all-done.1 = bf16[32,2,128,896]{3,2,1,0:T(8,128)(2,1)} async-done(((bf16[32,2,128,896]{3,2,1,0:T(8,128)(2,1)}), bf16[32,2,128,896]{3,2,1,0:T(8,128)(2,1)}, u32[]{:S(2)}, u32[]{:S(2)}) %all-to-all-start.1) | async-done | bytes 14680096 | tf_op jit(solution)/shard_map/all_to_all | solution.py:62
  241.5 9.1 %gather_fusion.1 = bf16[24,128,896]{2,1,0:T(8,128)(2,1)} fusion(bf16[64,128,896]{2,1,0:T(8,128)(2,1)} %bitcast.3, s32[1024]{0:T(1024)S(1)} %pad_clamp_fusion), kind=kCustom, calls=%fused_computation.1 | custom fusion | bytes 11010144 | tf_op jit(solution)/shard_map/gather | solution.py:69
  250.5 3.8 multiply_reduce_fusion
  254.4 10.4 %convolution_convert_fusion.1 = bf16[24,128,896]{2,1,0:T(8,128)(2,1)} fusion(f32[24,128]{1,0:T(8,128)S(1)} %add_rsqrt_fusion.2, bf16[24,128,896]{2,1,0:T(8,128)(2,1)} %gather_fusion.1, bf16[448,896]{1,0:T(8,128)(2,1)S(1)} %copy-done.4, bf16[896,448]{0,1:T(8,128)(2,1)S(1)} %copy-done.5), kind=kOutput, calls=%fused_computation.19 | convolution fusion | flops 4955897856 | bytes 12627968 | tf_op jit(solution)/shard_map/btf,fe->bte/dot_general | solution.py:78
  264.9 0.7 all-gather.5.cloned.1.call-update
  265.9 8.2 %convert_element_type.38 = f32[24,128,896]{2,1,0:T(8,128)} convert(bf16[24,128,896]{2,1,0:T(8,128)(2,1)} %gather_fusion.1) | non-fusion elementwise | flops 2752512 | bytes 16515072 | tf_op jit(solution)/shard_map/convert_element_type | solution.py:70
  274.0 90.7 %reduce-scatter.2.cloned.1.call-done = bf16[3,128,896]{2,1,0:T(8,128)(2,1)} async-done(((bf16[24,128,896]{2,1,0:T(8,128)(2,1)}), bf16[3,128,896]{2,1,0:T(8,128)(2,1)}) %reduce-scatter.2.cloned.1.call-update) | async-done | bytes 688144 | tf_op jit(solution)/shard_map/reduce_scatter | solution.py:77
  364.8 2.5 add_convert_fusion
  367.9 71.6 %all-gather.5.cloned.1.call-done = bf16[768,4096]{1,0:T(8,128)(2,1)} async-done(((bf16[768,512]{1,0:T(8,128)(2,1)}), bf16[768,4096]{1,0:T(8,128)(2,1)}) %all-gather.5.cloned.1.call-update) | async-done | bytes 6291472 | tf_op jit(solution)/shard_map/all_gather | solution.py:91
  439.5 7.1 %multiply_reduce_fusion.2 = (f32[768,4]{0,1:T(4,128)S(1)}, f32[768,512]{0,1:T(8,128)S(1)}) fusion(bf16[768,4096]{1,0:T(8,128)(2,1)} %all-gather.5.cloned.1.call-done, bf16[4096,512]{1,0:T(8,128)(2,1)} %param.13), kind=kOutput, calls=%fused_computation.33 | convolution fusion | flops 3222008832 | bytes 12070912 | tf_op jit(solution)/shard_map/dot_general | solution.py:90
  447.2 1.6 copy.49
  448.9 1.8 multiply_convert_fusion.3
  450.7 56.3 %all-gather.3.cloned.1.call-done = bf16[24,128,896]{2,1,0:T(8,128)(2,1)} async-done(((bf16[3,128,896]{2,1,0:T(8,128)(2,1)}), bf16[24,128,896]{2,1,0:T(8,128)(2,1)}) %all-gather.3.cloned.1.call-update) | async-done | bytes 5505040 | tf_op jit(solution)/shard_map/all_gather | solution.py:89
  507.0 8.6 %multiply_reduce_fusion.1 = (f32[3072,4]{0,1:T(4,128)S(1)}, f32[3072,4,128]{2,0,1:T(8,128)}) fusion(bf16[3072,896,1]{1,0,2:T(8,128)(2,1)} %bitcast.51, bf16[4,128,896]{2,1,0:T(8,128)(2,1)S(1)} %bitcast.49), kind=kOutput, calls=%fused_computation.6 | convolution fusion | flops 2821705728 | bytes 12763136 | tf_op jit(solution)/shard_map/dot_general | solution.py:97
  515.6 4.8 convolution_convert_fusion
  520.4 5.6 %reshape_reshape.3 = bf16[12,256,4,128]{3,2,1,0:T(4,128)(2,1)} reshape(bf16[3072,512]{1,0:T(8,128)(2,1)} %convolution_convert_fusion) | data formatting | bytes 6291456 | tf_op jit(solution)/shard_map/reshape;reshape | solution.py:30
  526.0 4.4 multiply_convert_fusion.1
  530.4 1.3 fusion.15
  532.3 1.2 fusion.26
  534.3 1.1 concatenate.7
  (41 shorter events, 3.9 us)
Async XLA Ops:
  6.5 509.1 %copy-start = (bf16[896,512]{1,0:T(8,128)(2,1)S(1)}, bf16[896,512]{1,0:T(8,128)(2,1)}, u32[]{:S(2)}) copy-start(bf16[896,512]{1,0:T(8,128)(2,1)} %param.15) | copy-start | bytes 2752516
  33.7 207.8 %all-to-all-start.1 = ((bf16[32,2,128,896]{3,2,1,0:T(8,128)(2,1)}), bf16[32,2,128,896]{3,2,1,0:T(8,128)(2,1)}, u32[]{:S(2)}, u32[]{:S(2)}) async-start(bf16[32,2,128,896]{3,2,1,0:T(8,128)(2,1)} %bitcast.42), calls=%async_computation.1 | async-start | bytes 29360128 | tf_op jit(solution)/shard_map/all_to_all | solution.py:62
  39.1 325.6 %reduce-scatter.2.cloned.1.call-start = ((), (), s32[]{:S(2)}) async-start(), calls=%async_computation.3 | async-start | bytes 6193152 | tf_op jit(solution)/shard_map/reduce_scatter | solution.py:77
  250.5 3.8 copy-start.4
  250.5 3.9 copy-start.5
  264.9 174.7 %all-gather.5.cloned.1.call-start = ((), (), s32[]{:S(2)}) async-start(), calls=%async_computation.5 | async-start | bytes 7077888 | tf_op jit(solution)/shard_map/all_gather | solution.py:91
  265.6 241.4 %all-gather.3.cloned.1.call-start = ((), (), s32[]{:S(2)}) async-start(), calls=%async_computation.4 | async-start | bytes 6193152 | tf_op jit(solution)/shard_map/all_gather | solution.py:89
  265.9 101.5 %copy-start.2 = (bf16[896,512]{1,0:T(8,128)(2,1)S(1)}, bf16[896,512]{1,0:T(8,128)(2,1)}, u32[]{:S(2)}) copy-start(bf16[896,512]{1,0:T(8,128)(2,1)} %param.14) | copy-start | bytes 2752516
  507.0 8.6 %copy-start.3 = (bf16[24,128,896]{2,1,0:T(8,128)(2,1)S(1)}, bf16[24,128,896]{2,1,0:T(8,128)(2,1)}, u32[]{:S(2)}) copy-start(bf16[24,128,896]{2,1,0:T(8,128)(2,1)} %all-gather.3.cloned.1.call-done) | copy-start | bytes 16515076
  530.4 1.9 copy-start.1
Sparse Core Ops, SparseCore 0:
  265.0 99.7 reduce-scatter.1
  366.6 72.9 all-gather.4
  441.3 65.6 all-gather.2
where the time goes:
time: 542 us
  waiting for transfers between devices  422 us (78%)
  matrix products  33.7 us (6%)
  local copies, waits for them, and re-layouts  31.3 us (6%)
  other arithmetic  20.9 us (4%)
  blocking collectives  15.3 us (3%)
  between operations  13.3 us (2%)
  starting transfers between devices  5.75 us (1%)
    all_to_all x1, waiting for transfers between devices, shards(): lax.all_to_all(database[lax.all_to_all(requests, 'dp', split_axis=0, conc...  202 us
    reduce_scatter x1, waiting for transfers between devices, shards(): lax.psum_scatter(jnp.einsum('btf,fe->bte', active, w_down, preferred_elem...  90.7 us
    all_gather x1, waiting for transfers between devices, shards(): lax.all_gather(hidden_states, 'tensor', axis=1, tiled=True)  71.6 us
    all_gather x1, waiting for transfers between devices, shards(): encoded = lax.all_gather(encoded_own, 'tensor', axis=0, tiled=True)  56.3 us
    all_to_all x1, blocking collectives, shards(): lax.all_to_all(requests, 'dp', split_axis=0, concat_axis=0, tiled=True)  15.3 us
  transfers between devices with their start and end apart: 4, of which 4 were waited for; matrix products, arithmetic and copies ran while one was open for 4% of the time, Pallas kernels for 0%

commit v1 on v0

--- a/solution.py
+++ b/solution.py
@@ -86,7 +86,14 @@
         raw_float, lax.axis_index("tensor") * own_blocks, own_blocks, 0
     )
     encoded_own = (raw_own + summed).astype(jnp.bfloat16)
-    encoded = lax.all_gather(encoded_own, "tensor", axis=0, tiled=True)
+    width = lax.axis_size("tensor")
+    encoded = lax.all_to_all(
+        jnp.tile(encoded_own, [width if pp == 0 else 1 for pp in range(encoded_own.ndim)]),
+        "tensor",
+        split_axis=0,
+        concat_axis=0,
+        tiled=True,
+    )
     projected = jnp.dot(
         lax.all_gather(hidden_states, "tensor", axis=1, tiled=True),
         w_query,

time: 542 us -> 604 us (1.11)
  waiting for transfers between devices: 422 us -> 473 us
    all_gather x1, waiting for transfers between devices: 71.6 us -> 179 us  [shards(): lax.all_gather(hidden_states, 'tensor', axis=1, tiled=True)]
    all_gather x1 -> x0, waiting for transfers between devices: 56.3 us -> none  [shards(): encoded = lax.all_gather(encoded_own, 'tensor', axis=0, tiled=True)]
  transfers between devices with their start and end apart: 4 -> 4, of which waited for: 4 -> 3; matrix products, arithmetic and copies ran while one was open for 4% -> 4% of each run, Pallas kernels for 0% -> 0%
where the time goes in v1:
time: 604 us; the launch traced here: 603 us
  waiting for transfers between devices  473 us (78%)
  matrix products  36 us (6%)
  local copies, waits for them, and re-layouts  34.5 us (6%)
  other arithmetic  20 us (3%)
  blocking collectives  15.3 us (3%)
  between operations  13.6 us (2%)
  starting transfers between devices  10.5 us (2%)
    all_to_all x1, waiting for transfers between devices, shards(): lax.all_to_all(database[lax.all_to_all(requests, 'dp', split_axis=0, conc...  202 us
    all_gather x1, waiting for transfers between devices, shards(): lax.all_gather(hidden_states, 'tensor', axis=1, tiled=True)  179 us
    reduce_scatter x1, waiting for transfers between devices, shards(): lax.psum_scatter(jnp.einsum('btf,fe->bte', active, w_down, preferred_elem...  91.1 us
    all_to_all x1, blocking collectives, shards(): lax.all_to_all(requests, 'dp', split_axis=0, concat_axis=0, tiled=True)  15.3 us
  transfers between devices with their start and end apart: 4, of which 3 were waited for; matrix products, arithmetic and copies ran while one was open for 4% of the time, Pallas kernels for 0%

profile of v1, /device:TPU:1, one launch (start us, length us, event | category | flops | bytes accessed | tf_op | source)
XLA Modules:
  0.0 603.0 jit_solution(15111456077777251626)
XLA Ops:
  6.5 0.8 copy.37
  8.0 15.3 %all_to_all.22 = s32[32,1,2]{2,1,0:T(1,128)S(1)} all-to-all(s32[32,1,2]{2,1,0:T(1,128)S(1)} %bitcast.52), channel_id=1, replica_groups=mesh['dp'=32,'tensor'=8] {'dp'}, dimensions={0} | all-to-all | bytes 512 | tf_op jit(solution)/shard_map/all_to_all | solution.py:63
  23.7 10.0 %gather_fusion = bf16[64,128,896]{2,1,0:T(8,128)(2,1)} fusion(bf16[16,128,896]{2,1,0:T(8,128)(2,1)} %param.10, s32[1024]{0:T(1024)S(1)} %pad_clamp_fusion.1), kind=kCustom, calls=%fused_computation | custom fusion | bytes 29360384 | tf_op jit(solution)/shard_map/gather | solution.py:63
  33.7 5.4 all-to-all-start.1
  39.3 202.2 %all-to-all-done.1 = bf16[32,2,128,896]{3,2,1,0:T(8,128)(2,1)} async-done(((bf16[32,2,128,896]{3,2,1,0:T(8,128)(2,1)}), bf16[32,2,128,896]{3,2,1,0:T(8,128)(2,1)}, u32[]{:S(2)}, u32[]{:S(2)}) %all-to-all-start.1) | async-done | bytes 14680096 | tf_op jit(solution)/shard_map/all_to_all | solution.py:62
  241.5 9.1 %gather_fusion.1 = bf16[24,128,896]{2,1,0:T(8,128)(2,1)} fusion(bf16[64,128,896]{2,1,0:T(8,128)(2,1)} %bitcast.3, s32[1024]{0:T(1024)S(1)} %pad_clamp_fusion), kind=kCustom, calls=%fused_computation.1 | custom fusion | bytes 11010144 | tf_op jit(solution)/shard_map/gather | solution.py:69
  250.6 3.8 multiply_reduce_fusion
  254.4 10.4 %convolution_convert_fusion.1 = bf16[24,128,896]{2,1,0:T(8,128)(2,1)} fusion(f32[24,128]{1,0:T(8,128)S(1)} %add_rsqrt_fusion.2, bf16[24,128,896]{2,1,0:T(8,128)(2,1)} %gather_fusion.1, bf16[448,896]{1,0:T(8,128)(2,1)S(1)} %copy-done.3, bf16[896,448]{0,1:T(8,128)(2,1)S(1)} %copy-done.4), kind=kOutput, calls=%fused_computation.19 | convolution fusion | flops 4955897856 | bytes 12627968 | tf_op jit(solution)/shard_map/btf,fe->bte/dot_general | solution.py:78
  265.6 8.1 %convert_element_type.38 = f32[24,128,896]{2,1,0:T(8,128)} convert(bf16[24,128,896]{2,1,0:T(8,128)(2,1)} %gather_fusion.1) | non-fusion elementwise | flops 2752512 | bytes 16515072 | tf_op jit(solution)/shard_map/convert_element_type | solution.py:70
  273.7 91.1 %reduce-scatter.2.cloned.1.call-done = bf16[3,128,896]{2,1,0:T(8,128)(2,1)} async-done(((bf16[24,128,896]{2,1,0:T(8,128)(2,1)}), bf16[3,128,896]{2,1,0:T(8,128)(2,1)}) %reduce-scatter.2.cloned.1.call-update) | async-done | bytes 688144 | tf_op jit(solution)/shard_map/reduce_scatter | solution.py:77
  364.8 1.7 add_convert_fusion
  366.4 3.2 tile.4
  369.6 5.0 all-to-all-start.2
  375.2 179.1 %all-gather.2.cloned.1.call-done = bf16[768,4096]{1,0:T(8,128)(2,1)} async-done(((bf16[768,512]{1,0:T(8,128)(2,1)}), bf16[768,4096]{1,0:T(8,128)(2,1)}) %all-gather.2.cloned.1.call-update) | async-done | bytes 6291472 | tf_op jit(solution)/shard_map/all_gather | solution.py:98
  554.3 7.1 %multiply_reduce_fusion.2 = (f32[768,4]{0,1:T(4,128)S(1)}, f32[768,512]{0,1:T(8,128)S(1)}) fusion(bf16[768,4096]{1,0:T(8,128)(2,1)} %all-gather.2.cloned.1.call-done, bf16[4096,512]{1,0:T(8,128)(2,1)} %param.13), kind=kOutput, calls=%fused_computation.33 | convolution fusion | flops 3222008832 | bytes 12070912 | tf_op jit(solution)/shard_map/dot_general | solution.py:97
  561.9 1.6 copy.49
  563.7 1.8 multiply_convert_fusion.3
  565.6 8.2 %multiply_reduce_fusion.1 = (f32[3072,4]{0,1:T(4,128)S(1)}, f32[3072,4,128]{2,0,1:T(8,128)}) fusion(bf16[3072,896,1]{1,0,2:T(8,128)(2,1)} %bitcast.12, bf16[4,128,896]{2,1,0:T(8,128)(2,1)S(1)} %bitcast.51), kind=kOutput, calls=%fused_computation.6 | convolution fusion | flops 2821705728 | bytes 12763136 | tf_op jit(solution)/shard_map/dot_general | solution.py:104
  573.8 7.4 %convolution_convert_fusion = bf16[3072,512]{1,0:T(8,128)(2,1)} fusion(bf16[3072,896]{1,0:T(8,128)(2,1)} %bitcast.9, bf16[896,512]{1,0:T(8,128)(2,1)S(1)} %copy-done), kind=kOutput, calls=%fused_computation.18 | convolution fusion | flops 2820145152 | bytes 9568256 | tf_op jit(solution)/shard_map/dot_general | solution.py:105
  581.2 5.5 reshape_reshape.3
  586.7 4.4 multiply_convert_fusion.1
  591.2 1.3 fusion.15
  593.1 1.2 fusion.26
  595.1 1.1 concatenate.7
  (39 shorter events, 4.4 us)
Async XLA Ops:
  6.5 567.2 %copy-start = (bf16[896,512]{1,0:T(8,128)(2,1)S(1)}, bf16[896,512]{1,0:T(8,128)(2,1)}, u32[]{:S(2)}) copy-start(bf16[896,512]{1,0:T(8,128)(2,1)} %param.15) | copy-start | bytes 2752516
  33.7 207.8 %all-to-all-start.1 = ((bf16[32,2,128,896]{3,2,1,0:T(8,128)(2,1)}), bf16[32,2,128,896]{3,2,1,0:T(8,128)(2,1)}, u32[]{:S(2)}, u32[]{:S(2)}) async-start(bf16[32,2,128,896]{3,2,1,0:T(8,128)(2,1)} %bitcast.43), calls=%async_computation.1 | async-start | bytes 29360128 | tf_op jit(solution)/shard_map/all_to_all | solution.py:62
  39.1 325.6 %reduce-scatter.2.cloned.1.call-start = ((), (), s32[]{:S(2)}) async-start(), calls=%async_computation.4 | async-start | bytes 6193152 | tf_op jit(solution)/shard_map/reduce_scatter | solution.py:77
  250.6 3.8 copy-start.3
  250.6 3.9 copy-start.4
  264.9 289.5 %all-gather.2.cloned.1.call-start = ((), (), s32[]{:S(2)}) async-start(), calls=%async_computation.5 | async-start | bytes 7077888 | tf_op jit(solution)/shard_map/all_gather | solution.py:98
  369.6 5.0 copy-start.2
  369.6 195.9 %all-to-all-start.2 = ((bf16[24,128,896]{2,1,0:T(8,128)(2,1)}), bf16[24,128,896]{2,1,0:T(8,128)(2,1)}, u32[]{:S(2)}, u32[]{:S(2)}) async-start(bf16[24,128,896]{2,1,0:T(8,128)(2,1)} %bitcast.44), calls=%async_computation.3 | async-start | bytes 11010048 | tf_op jit(solution)/shard_map/all_to_all | solution.py:90
  591.2 1.9 copy-start.1
Sparse Core Ops, SparseCore 0:
  265.0 99.7 reduce-scatter.1
  366.6 187.7 all-gather.1
